TPU v7x, 32 devices: a whole 2x2x4 slice. The times are simulated.
32 devices in a mesh: tm: 2 (over x), state: 16 (over z, y, core).
Axes of the slice: x: 2, y: 2, z: 4, core: 2. Of those that a mesh axis runs over, the one named last changes fastest.
Arguments:
- anomalies: bfloat16 [4, 24576, 256], P('tm', 'state'), may hold values from -23 to 23, as said below
- obs_weight: float32 [4, 24576], P('tm', 'state'), may hold values from 0.05 to 6, as said below
Outputs:
- smoothed: bfloat16 [4, 24576, 256], P('tm', 'state')
- suffix: float32 [4, 256, 256], P('tm')
Inputs may be any that keep to these rules, and one draw needn't show every extreme that they name: Member anomalies of order one, with member columns correlated. `obs_weight`: positive weights.
All inputs are finite; a program needn't handle non-finite values. Where the computation divides by a largest or mean magnitude, that divisor is 1e-20 or more.
Results may differ from a plain program's by a relative error of at most 0.001.
The roundings to bfloat16 on the way count: a program that leaves them out, or rounds other values in their place, can miss the bound.
Values sent between devices are 32-bit elements; how exact they have to be, the bound alone decides.
No kernel may reach another device: no remote copies, remote signals or barrier semaphores. Data moves between devices by JAX's collectives and lax.ppermute only.
A program may use at most 64 MiB of HBM per device.

v0:
```python
import jax
import jax.numpy as jnp
from jax import lax
from jax.sharding import PartitionSpec as P

NS_STEPS = 4


def carried_in(value, axis, join, neutral):
    count, mine = (lax.axis_size(axis), lax.axis_index(axis))
    pieces = lax.all_gather(value, axis)
    pieces = pieces[::-1]
    mine = count - 1 - mine
    so_far = jnp.full_like(value, 0) + jnp.asarray(neutral, value.dtype)

    def hop(position, so_far):
        longer = join(so_far, pieces[position])
        return jnp.where(position < mine, longer, so_far)

    return lax.fori_loop(0, count - 1, hop, so_far)


def newton_root(covariance):
    identity = jnp.eye(covariance.shape[-1], dtype=jnp.float32)
    row_bound = jnp.max(jnp.sum(jnp.abs(covariance), axis=-1), axis=-1)
    iterate = covariance / row_bound[:, None, None]
    inverse_root = jnp.broadcast_to(identity, covariance.shape)
    for sweep_index in range(NS_STEPS):
        factor = 1.5 * identity - 0.5 * jnp.matmul(
            inverse_root, iterate, precision=lax.Precision.HIGHEST
        )
        iterate = jnp.matmul(iterate, factor, precision=lax.Precision.HIGHEST)
        inverse_root = jnp.matmul(factor, inverse_root, precision=lax.Precision.HIGHEST)
    return inverse_root / jnp.sqrt(row_bound)[:, None, None]


def combine(earlier, later):
    return jnp.matmul(later, earlier, precision=lax.Precision.HIGHEST)


def on_device(anomalies, obs_weight):
    times_dev, rows_dev, members = anomalies.shape
    total_rows = rows_dev * lax.axis_size("state")
    weighted = (anomalies * obs_weight[:, :, None]).astype(jnp.bfloat16)
    partial_gram = jnp.einsum(
        "trm,trn->tmn", weighted, weighted, preferred_element_type=jnp.float32
    )
    gram_sum = lax.psum(partial_gram, "state")
    covariance = gram_sum / total_rows + jnp.eye(members, dtype=jnp.float32)
    transform = newton_root(covariance)
    local_product = transform[times_dev - 1]
    time_index = 0
    local_product = jnp.matmul(
        transform[time_index], local_product, precision=lax.Precision.HIGHEST
    )
    identity = jnp.eye(members, dtype=jnp.float32)
    remote = carried_in(local_product, "tm", combine, identity)
    product = remote
    suffixes = []
    for time_index in range(times_dev - 1, -1, -1):
        product = jnp.matmul(transform[time_index], product, precision=lax.Precision.HIGHEST)
        suffixes.append(product)
    suffix = jnp.stack(suffixes[::-1])
    smoothed = jnp.einsum(
        "trm,tmn->trn", anomalies, suffix.astype(jnp.bfloat16), preferred_element_type=jnp.float32
    ).astype(jnp.bfloat16)
    return (smoothed, suffix)


def solution(mesh):
    placed = (P("tm", "state", None), P("tm", "state"))
    return jax.shard_map(
        on_device,
        mesh=mesh,
        in_specs=placed,
        out_specs=(P("tm", "state", None), P("tm", None, None)),
        check_vma=False,
    )
```

profile of v0, /device:TPU:0, one launch (start us, length us, event | category | flops | bytes accessed | tf_op | source)
XLA Modules:
  0.0 135.0 jit_solution(14095974973290434030)
XLA Ops:
  7.2 0.0 all-reduce.2.cloned.1.call-start
  7.2 4.3 %fusion.1 = f32[2,256,256]{2,1,0:T(8,128)} fusion(bf16[2,1536,256]{2,1,0:T(8,128)(2,1)} %param.2, f32[2,1536]{1,0:T(2,128)} %param.3), kind=kOutput, calls=%fused_computation.3 | convolution fusion | flops 405012480 | bytes 2109440 | tf_op jit(solution)/shard_map/trm,trn->tmn/dot_general | solution.py:45
  11.5 0.0 all-reduce.2.cloned.1.call-update
  11.6 93.2 %all-reduce.2.cloned.1.call-done = f32[2,256,256]{2,1,0:T(8,128)} async-done(((f32[2,256,256]{2,1,0:T(8,128)}), f32[2,256,256]{2,1,0:T(8,128)}) %all-reduce.2.cloned.1.call-update) | async-done | bytes 524304 | tf_op jit(solution)/shard_map/psum | solution.py:48
  104.9 1.2 abs_reduce_fusion
  106.1 0.1 reduce_max.9
  106.2 0.0 copy-start.2
  106.2 1.8 %fusion.6 = f32[2,256,256]{2,1,0:T(8,128)S(1)} fusion(f32[256,256]{1,0:T(8,128)S(1)} %fusion.13, f32[256,256]{1,0:T(8,128)S(1)} %fusion.14, f32[2,256,256]{2,1,0:T(8,128)} %all-reduce.2.cloned.1.call-done, f32[2]{0:T(128)S(1)} %reduce_max.9), kind=kOutput, calls=%fused_computation.13 | convolution fusion | flops 403308544 | bytes 1572872 | tf_op jit(solution)/shard_map/dot_general | solution.py:29
  108.0 0.6 fusion.10
  108.7 0.0 copy-done.2
  108.7 0.7 fusion.17
  109.4 0.7 fusion.5
  110.1 0.7 fusion.23
  110.7 0.7 fusion.22
  111.4 0.7 fusion.4
  112.1 0.7 fusion.24
  112.7 0.7 fusion.25
  113.4 0.7 fusion.3
  114.0 0.7 convolution_divide_fusion
  114.7 0.4 fusion.15
  115.1 9.4 %all-gather = f32[512,256]{1,0:T(8,128)S(1)} all-gather(f32[256,256]{1,0:T(8,128)S(1)} %fusion.15), channel_id=2, replica_groups=mesh['tm'=2,'state'=16] {'tm'}, dimensions={0}, use_global_device_ids=true | all-gather | bytes 786432 | tf_op jit(solution)/shard_map/all_gather | solution.py:11
  124.4 0.0 copy-start.1
  124.4 0.3 convolution_select_fusion
  124.7 0.4 fusion.16
  125.1 0.4 convolution_bitcast_fusion
  125.6 0.3 copy-done.1
  125.9 0.0 copy-start
  125.9 0.7 fusion
  126.5 0.1 copy-done
  126.6 1.6 %copy.9 = bf16[2,1536,256]{2,1,0:T(8,128)(2,1)} copy(bf16[2,1536,256]{1,2,0:T(8,128)(2,1)S(1)} %fusion) | data formatting | bytes 3145728
  (4 shorter events, 0.1 us)
Async XLA Ops:
  7.2 97.7 %all-reduce.2.cloned.1.call-start = ((), (), s32[]{:S(2)}) async-start(), calls=%async_computation | async-start | bytes 1048576 | tf_op jit(solution)/shard_map/psum | solution.py:48
  106.2 2.5 %copy-start.2 = (f32[2,256,256]{2,1,0:T(8,128)S(1)}, f32[2,256,256]{2,1,0:T(8,128)}, u32[]{:S(2)}) copy-start(f32[2,256,256]{2,1,0:T(8,128)} %all-reduce.2.cloned.1.call-done) | copy-start | bytes 1572868
  124.4 1.4 %copy-start.1 = (bf16[2,1536,256]{2,1,0:T(8,128)(2,1)S(1)}, bf16[2,1536,256]{2,1,0:T(8,128)(2,1)}, u32[]{:S(2)}) copy-start(bf16[2,1536,256]{2,1,0:T(8,128)(2,1)} %param.2) | copy-start | bytes 4718596
  125.9 0.8 copy-start
Sparse Core Ops, SparseCore 0:
  12.0 92.8 all-reduce.1
where the time goes:
time: 135 us
  waiting for transfers between devices  93.3 us (69%)
  matrix products  14.8 us (11%)
  between operations  14.2 us (11%)
  blocking collectives  9.35 us (7%)
  local copies, waits for them, and re-layouts  1.98 us (1%)
  other arithmetic  1.4 us (1%)
    psum x1, waiting for transfers between devices, on_device(): gram_sum = lax.psum(partial_gram, 'state')  93.2 us
    all_gather x1, blocking collectives, carried_in(): pieces = lax.all_gather(value, axis)  9.35 us
    dot_general x1, matrix products, on_device(): jnp.einsum('trm,trn->tmn', weighted, weighted, preferred_element_type=jnp...  4.31 us
    dot_general x4, matrix products, newton_root(): jnp.matmul(inverse_root, iterate, precision=lax.Precision.HIGHEST)  3.79 us
  transfers between devices with their start and end apart: 1, of which 1 were waited for; matrix products, arithmetic and copies ran while one was open for 0% of the time, Pallas kernels for 0%

commit v1 on v0

--- a/solution.py
+++ b/solution.py
@@ -2,6 +2,7 @@
 import jax.numpy as jnp
 from jax import lax
 from jax.sharding import PartitionSpec as P
+from jax.lax import all_gather
 
 NS_STEPS = 4
 
@@ -45,7 +46,8 @@
     partial_gram = jnp.einsum(
         "trm,trn->tmn", weighted, weighted, preferred_element_type=jnp.float32
     )
-    gram_sum = lax.psum(partial_gram, "state")
+    track_column_here = lambda values: jnp.sum(all_gather(values, "state"), axis=0)
+    gram_sum = track_column_here(partial_gram)
     covariance = gram_sum / total_rows + jnp.eye(members, dtype=jnp.float32)
     transform = newton_root(covariance)
     local_product = transform[times_dev - 1]

time: 135 us -> 121 us (0.90)
  waiting for transfers between devices: 93.3 us -> 77.7 us
  other arithmetic: 1.4 us -> 4.34 us
    psum x1 -> x0, waiting for transfers between devices: 93.2 us -> none  [on_device(): gram_sum = lax.psum(partial_gram, 'state')]
    all_gather x0 -> x1, waiting for transfers between devices: none -> 77.7 us  [on_device(): all_gather(values, 'state')]
    reduce_sum x0 -> x1, other arithmetic: none -> 3.98 us  [on_device(): jnp.sum(all_gather(values, 'state'), axis=0)]
where the time goes in v1:
time: 121 us
  waiting for transfers between devices  77.7 us (64%)
  between operations  14.2 us (12%)
  matrix products  13.7 us (11%)
  blocking collectives  9.15 us (8%)
  other arithmetic  4.34 us (4%)
  local copies, waits for them, and re-layouts  1.98 us (2%)
    all_gather x1, waiting for transfers between devices, on_device(): all_gather(values, 'state')  77.7 us
    all_gather x1, blocking collectives, carried_in(): pieces = lax.all_gather(value, axis)  9.15 us
    dot_general x1, matrix products, on_device(): jnp.einsum('trm,trn->tmn', weighted, weighted, preferred_element_type=jnp...  4.32 us
    reduce_sum x1, other arithmetic, on_device(): jnp.sum(all_gather(values, 'state'), axis=0)  3.98 us
    dot_general x4, matrix products, newton_root(): jnp.matmul(inverse_root, iterate, precision=lax.Precision.HIGHEST)  2.68 us
    dot_general x4, matrix products, newton_root(): jnp.matmul(factor, inverse_root, precision=lax.Precision.HIGHEST)  2.59 us
  transfers between devices with their start and end apart: 1, of which 1 were waited for; matrix products, arithmetic and copies ran while one was open for 0% of the time, Pallas kernels for 0%

profile of v1, /device:TPU:0, one launch (start us, length us, event | category | flops | bytes accessed | tf_op | source)
XLA Modules:
  0.0 121.1 jit_solution(1492839329790061692)
XLA Ops:
  7.2 0.0 all-gather.4.cloned.1.call-start
  7.2 4.3 %fusion.1 = f32[2,256,256]{2,1,0:T(8,128)} fusion(bf16[2,1536,256]{2,1,0:T(8,128)(2,1)} %param.2, f32[2,1536]{1,0:T(2,128)} %param.3), kind=kOutput, calls=%fused_computation.3 | convolution fusion | flops 405012480 | bytes 2109440 | tf_op jit(solution)/shard_map/trm,trn->tmn/dot_general | solution.py:46
  11.5 0.0 all-gather.4.cloned.1.call-update
  11.6 77.7 %all-gather.4.cloned.1.call-done = f32[32,256,256]{2,1,0:T(8,128)} async-done(((f32[2,256,256]{2,1,0:T(8,128)}), f32[32,256,256]{2,1,0:T(8,128)}) %all-gather.4.cloned.1.call-update) | async-done | bytes 8388624 | tf_op jit(solution)/shard_map/all_gather | solution.py:49
  89.3 4.0 %reduce_sum.18 = f32[2,256,256]{2,1,0:T(8,128)S(1)} reduce(f32[16,2,256,256]{3,2,1,0:T(8,128)} %bitcast.35, f32[]{:T(128)} %constant.10.clone.1), dimensions={0}, to_apply=%region_0.0 | reduce | flops 1966080 | bytes 8912900 | tf_op jit(solution)/shard_map/reduce_sum | solution.py:49
  93.3 0.2 abs_reduce_fusion
  93.5 0.1 reduce_max.9
  93.6 0.7 fusion.6
  94.3 0.7 fusion.17
  95.0 0.6 fusion.10
  95.7 0.7 fusion.5
  96.3 0.7 fusion.23
  97.0 0.7 fusion.22
  97.7 0.7 fusion.4
  98.3 0.7 fusion.25
  99.0 0.7 fusion.24
  99.7 0.7 fusion.3
  100.3 0.7 convolution_divide_fusion
  101.0 0.4 fusion.15
  101.4 9.2 %all-gather.1 = f32[512,256]{1,0:T(8,128)S(1)} all-gather(f32[256,256]{1,0:T(8,128)S(1)} %fusion.15), channel_id=3, replica_groups=mesh['tm'=2,'state'=16] {'tm'}, dimensions={0}, use_global_device_ids=true | all-gather | bytes 786432 | tf_op jit(solution)/shard_map/all_gather | solution.py:12
  110.5 0.0 copy-start.1
  110.5 0.3 convolution_select_fusion
  110.8 0.4 fusion.16
  111.2 0.4 convolution_bitcast_fusion
  111.6 0.3 copy-done.1
  111.9 0.0 copy-start
  111.9 0.7 fusion
  112.6 0.1 copy-done
  112.7 1.6 %copy.12 = bf16[2,1536,256]{2,1,0:T(8,128)(2,1)} copy(bf16[2,1536,256]{1,2,0:T(8,128)(2,1)S(1)} %fusion) | data formatting | bytes 3145728
  (4 shorter events, 0.1 us)
Async XLA Ops:
  7.2 82.1 %all-gather.4.cloned.1.call-start = ((), (), s32[]{:S(2)}) async-start(), calls=%async_computation | async-start | bytes 8912896 | tf_op jit(solution)/shard_map/all_gather | solution.py:49
  110.5 1.4 %copy-start.1 = (bf16[2,1536,256]{2,1,0:T(8,128)(2,1)S(1)}, bf16[2,1536,256]{2,1,0:T(8,128)(2,1)}, u32[]{:S(2)}) copy-start(bf16[2,1536,256]{2,1,0:T(8,128)(2,1)} %param.2) | copy-start | bytes 4718596
  111.9 0.8 copy-start
Sparse Core Ops, SparseCore 0:
  11.7 77.5 all-gather.3
